TPU v7x, 32 devices: a whole 2x2x4 slice. The times are simulated.
32 devices in a mesh: lines: 2 (over x), col: 16 (over z, y, core).
Axes of the slice: x: 2, y: 2, z: 4, core: 2. Of those that a mesh axis runs over, the one named last changes fastest.
Arguments:
- primary: float32 [16, 4, 128, 256], P(None, 'lines', 'col'), parts along dimension 1, may hold values from -6 to 6
- conductivity: float32 [128, 512], P('col', 'lines'), parts along dimension 1, may hold values from 0.1 to 10
- wavenumbers: float32 [16], replicated, may hold values from 0.05 to 1.5
- quadrature: float32 [16], replicated, may hold values from 0.02 to 0.2
- electrodes: int32 [64], P(('lines', 'col')), parts along dimension 0, may hold values from 0 to 127, as said below
- far_pole: int32 [4, 32], P('lines'), parts along dimension 0, may hold values from 0 to 31, as said below
- observed: float32 [4, 32], P('lines'), parts along dimension 0, may hold values from -6 to 6
- prior_adjoint: float32 [16, 4, 128, 256], P(None, 'lines', 'col'), parts along dimension 1, may hold values from -0.012 to 0.012
Outputs:
- predicted: float32 [4, 32], P('lines'), parts along dimension 0
- gradient: float32 [128, 512], P('col', 'lines'), parts along dimension 1
There are 2 independent parts, one for each index of `lines`. A program takes and returns all parts, laid end to end along the dimension named above; an argument that names none is the same for every part. Nothing has to cross between parts.
Inputs may be any that keep to these rules, and one draw needn't show every extreme that they name: electrodes[e] lies in columns 4 e to 4 e + 3. far_pole[s, r] differs from r by 1 to 8.
All inputs are finite; a program needn't handle non-finite values.
Results may differ from a plain program's by a relative error of at most 0.0003.
Values sent between devices are 32-bit elements; how exact they have to be, the bound alone decides.
No kernel may reach another device: no remote copies, remote signals or barrier semaphores. Data moves between devices by JAX's collectives and lax.ppermute only.
A program may use at most 64 MiB of HBM per device.

v0:
```python
import math
import jax
import jax.numpy as jnp
from jax import lax
from jax.sharding import Mesh
from jax.sharding import PartitionSpec as P

ITERS = 2


def halo(block, axis, dim, width):
    count = lax.axis_size(axis)
    edge_shape = list(block.shape)
    edge_shape[dim] = width
    if count == 1:
        zeros = jnp.zeros(edge_shape, block.dtype)
        return jnp.concatenate([zeros, block, zeros], axis=dim)
    forward = [(i, i + 1) for i in range(count - 1)]
    backward = [(target, source) for source, target in forward]
    low = lax.ppermute(
        lax.slice_in_dim(block, block.shape[dim] - width, None, axis=dim), axis, forward
    )
    high = lax.ppermute(lax.slice_in_dim(block, 0, width, axis=dim), axis, backward)
    return jnp.concatenate([low, block, high], axis=dim)


def next_column(field, axis):
    count = lax.axis_size(axis)
    if count == 1:
        edge = jnp.zeros_like(field[:, :, :1])
    else:
        edge = lax.ppermute(field[:, :, :1], axis, [(i + 1, i) for i in range(count - 1)])
    return jnp.concatenate([field[:, :, 1:], edge], axis=2)


def coefficients(sigma_wide):
    center = sigma_wide[1:-1]
    west_face = 0.5 * (center + sigma_wide[:-2])
    east_face = 0.5 * (center + sigma_wide[2:])
    below_sigma = jnp.concatenate([center[:, 1:], jnp.zeros_like(center[:, :1])], axis=1)
    lower_face = 0.5 * (center + below_sigma)
    above_sigma = jnp.concatenate([jnp.zeros_like(center[:, :1]), center[:, :-1]], axis=1)
    upper_face = 0.5 * (center + above_sigma)
    top_row = jnp.arange(center.shape[1]) == 0
    upper_face = jnp.where(top_row[None, :], 0.0, upper_face)
    return (west_face, east_face, lower_face, upper_face, center)


def stencil(field_wide, faces_set, mass_scale):
    west_face, east_face, lower_face, upper_face, center = faces_set
    middle = field_wide[..., 1:-1, :]
    below_cells = jnp.concatenate([middle[..., 1:], jnp.zeros_like(middle[..., :1])], axis=-1)
    above_cells = jnp.concatenate([jnp.zeros_like(middle[..., :1]), middle[..., :-1]], axis=-1)
    result = west_face * (middle - field_wide[..., :-2, :]) + east_face * (
        middle - field_wide[..., 2:, :]
    )
    result = result + lower_face * (middle - below_cells) + upper_face * (middle - above_cells)
    return result + mass_scale * center * middle


def on_device(
    primary, conductivity, wavenumbers, quadrature, electrodes, far_pole, observed, prior_adjoint
):
    groups = lax.axis_size("kq")
    spread = lax.axis_size("cs")
    waves, sources, own_columns, depth = primary.shape
    per_group = waves // groups
    group = lax.axis_index("kq")
    block = lax.axis_index("cs")
    fields = per_group * sources

    def by_group(array):
        return array.reshape(groups, fields, own_columns, depth)

    sigma_copies = jnp.broadcast_to(conductivity[None, None], (groups, 1, own_columns, depth))
    send = jnp.concatenate([by_group(primary), by_group(prior_adjoint), sigma_copies], axis=1)
    if groups > 1:
        send = lax.all_to_all(send, "kq", 0, 2, tiled=True)
    received = send[0]
    width = groups * own_columns
    primary = received[:fields].reshape(per_group, sources, width, depth)
    prior_adjoint = received[fields : 2 * fields].reshape(per_group, sources, width, depth)
    sigma = received[2 * fields]
    columns = width * spread
    offset = block * width
    wide_sigma = halo(sigma, "cs", 0, 2)
    positions = offset - 2 + jnp.arange(width + 4)
    inside = (positions >= 0) & (positions < columns)
    contrast_wide = jnp.where(inside[:, None], wide_sigma - 1.0, 0.0)
    own_waves = lax.dynamic_slice_in_dim(wavenumbers, group * per_group, per_group)
    weights = lax.dynamic_slice_in_dim(quadrature, group * per_group, per_group)
    mass_scale = (own_waves * own_waves)[:, None, None, None]
    operator_faces = coefficients(wide_sigma[1:-1])

    def operate(state):
        return stencil(halo(state, "cs", 2, 1), operator_faces, mass_scale)

    def dots(left, right):
        total = jnp.sum(left * right, axis=(2, 3))
        if spread > 1:
            total = lax.psum(total, "cs")
        return total[:, :, None, None]

    def conjugate(source, start):
        if start is None:
            solution = jnp.zeros_like(source)
            residual = source
        else:
            solution = start
            residual = source - operate(start)
        direction = residual
        norm_now = dots(residual, residual)
        for iteration in range(ITERS):
            applied = operate(direction)
            step_size = norm_now / dots(direction, applied)
            solution = solution + step_size * direction
            if iteration + 1 < ITERS:
                residual = residual - step_size * applied
                norm_next = dots(residual, residual)
                direction = residual + norm_next / norm_now * direction
                norm_now = norm_next
        return solution

    source = -stencil(halo(primary, "cs", 2, 1), coefficients(contrast_wide[1:-1]), mass_scale)
    total_field = primary + conjugate(source, None)
    surface = total_field[:, :, :, 0]
    weighted = jnp.sum(weights[:, None, None] * surface, axis=0)
    packet = jnp.concatenate([weighted.reshape(-1), electrodes.astype(jnp.float32)])
    gathered = lax.all_gather(packet, ("cs", "kq"))
    partial = gathered[:, : sources * width].reshape(spread, groups, sources, width)
    line_surface = jnp.sum(partial, axis=1).transpose(1, 0, 2).reshape(sources, columns)
    all_electrodes = gathered[:, sources * width :].reshape(-1).astype(jnp.int32)
    count = all_electrodes.shape[0]
    picks = (all_electrodes[:, None] == jnp.arange(columns)[None, :]).astype(jnp.float32)
    potentials = jnp.sum(line_surface[:, None, :] * picks[None], axis=2)
    pole_hits = (far_pole[:, :, None] == jnp.arange(count)[None, None, :]).astype(jnp.float32)
    far_potentials = jnp.sum(potentials[:, None, :] * pole_hits, axis=2)
    predicted = potentials - far_potentials
    misfit = predicted - observed
    returned = jnp.sum(misfit[:, :, None] * pole_hits, axis=1)
    charge = misfit - returned
    own_picks = (all_electrodes[:, None] == offset + jnp.arange(width)[None, :]).astype(jnp.float32)
    charge_cols = jnp.sum(charge[:, :, None] * own_picks[None], axis=1)
    surface_row = (jnp.arange(depth) == 0).astype(jnp.float32)
    adjoint_source = weights[:, None, None, None] * charge_cols[None, :, :, None] * surface_row
    adjoint = conjugate(adjoint_source, prior_adjoint)
    adjoint_next = next_column(adjoint, "cs")
    total_next = next_column(total_field, "cs")
    adjoint_down = jnp.concatenate([adjoint[..., 1:], jnp.zeros_like(adjoint[..., :1])], axis=-1)
    total_down = jnp.concatenate(
        [total_field[..., 1:], jnp.zeros_like(total_field[..., :1])], axis=-1
    )
    correlation = (adjoint_next - adjoint) * (total_next - total_field)
    correlation = correlation + (adjoint_down - adjoint) * (total_down - total_field)
    correlation = correlation + mass_scale * adjoint * total_field
    gradient = jnp.sum(correlation, axis=(0, 1))
    if groups > 1:
        gradient = lax.psum_scatter(gradient, "kq", scatter_dimension=0, tiled=True)
    return (predicted, gradient)


def solution(mesh):
    lines = mesh.shape["lines"]
    col = mesh.shape["col"]

    def run(*arrays):
        groups = math.gcd(col, arrays[0].shape[0])
        split = Mesh(mesh.devices.reshape(lines, col // groups, groups), ("lines", "cs", "kq"))
        cells = ("cs", "kq")
        placed = (
            P(None, "lines", cells, None),
            P(cells, "lines"),
            P(),
            P(),
            P(("lines",) + cells),
            P("lines", None),
            P("lines", None),
            P(None, "lines", cells, None),
        )
        return jax.shard_map(
            on_device,
            mesh=split,
            in_specs=placed,
            out_specs=(P("lines", None), P(cells, "lines")),
            check_vma=False,
        )(*arrays)

    return run
```

profile of v0, /device:TPU:0, one launch (start us, length us, event | category | flops | bytes accessed | tf_op | source)
XLA Modules:
  0.0 163.5 jit_solution(5212997132904193159)
XLA Ops:
  7.2 0.7 broadcast_in_dim.34
  7.9 1.9 %pad_maximum_fusion = f32[16,5,8,256]{3,2,1,0:T(8,128)} fusion(f32[16,1,8,256]{3,2,1,0:T(8,128)S(1)} %broadcast_in_dim.34, f32[16,2,8,256]{3,2,1,0:T(8,128)} %param.15, f32[16,2,8,256]{3,2,1,0:T(8,128)} %param.8), kind=kLoop, calls=%fused_computation | loop fusion | flops 327680 | bytes 1310720 | tf_op jit(solution)/shard_map/concatenate | solution.py:76
  9.8 7.4 %all-to-all-start = ((f32[16,5,8,256]{3,2,1,0:T(8,128)}), f32[16,5,8,256]{3,2,1,0:T(8,128)S(1)}, u32[]{:S(2)}, u32[]{:S(2)}) async-start(f32[16,5,8,256]{3,2,1,0:T(8,128)} %pad_maximum_fusion), calls=%async_computation | async-start | bytes 1310720 | tf_op jit(solution)/shard_map/all_to_all | solution.py:78
  17.3 0.6 copy-done.2
  17.9 0.6 dynamic_slice.7
  19.8 0.6 dynamic_slice.6
  20.4 0.7 copy-done.4
  21.1 0.7 copy-done.5
  21.8 0.6 dynamic-slice
  23.0 10.8 %all-to-all-done = f32[16,5,8,256]{3,2,1,0:T(8,128)S(1)} async-done(((f32[16,5,8,256]{3,2,1,0:T(8,128)}), f32[16,5,8,256]{3,2,1,0:T(8,128)S(1)}, u32[]{:S(2)}, u32[]{:S(2)}) %all-to-all-start) | async-done | bytes 655392 | tf_op jit(solution)/shard_map/all_to_all | solution.py:78
  34.3 0.2 fusion.70
  34.5 0.1 fusion.60
  34.6 0.2 fusion.66
  34.8 0.1 fusion.72
  35.0 0.3 multiply_reduce_fusion.4
  35.3 0.2 multiply_reduce_fusion.3
  35.5 0.1 multiply_add_fusion.2
  35.8 0.3 fusion.52
  36.2 0.7 fusion.58
  37.1 60.8 %all-reduce.34 = f32[4128]{0:T(1024)S(1)} all-reduce(f32[4128]{0:T(1024)S(1)} %maximum_dynamic-update-slice_fusion), channel_id=2, replica_groups=mesh['lines'=2,'col'=16] {'col'}, use_global_device_ids=true, to_apply=%add.34 | all-reduce | flops 4128 | bytes 33024
  98.3 0.6 copy-done
  98.8 0.2 select_reduce_fusion.1
  99.0 0.5 copy-done.1
  99.5 0.6 fusion.64
  100.3 0.6 broadcast_multiply_fusion.1
  100.9 0.2 fusion.31
  101.3 0.3 multiply_reduce_fusion.1
  101.6 0.2 multiply_reduce_fusion
  101.9 0.1 fusion.68
  102.1 0.3 fusion.51
  102.8 0.8 add_reduce_fusion
  103.6 53.0 %reduce-scatter.2.cloned.1.call-done = f32[8,256]{1,0:T(8,128)} async-done(((f32[128,256]{1,0:T(8,128)}), f32[8,256]{1,0:T(8,128)}) %reduce-scatter.2.cloned.1.call-update) | async-done | bytes 8208 | tf_op jit(solution)/shard_map/reduce_scatter | solution.py:158
  (47 shorter events, 2.1 us)
Async XLA Ops:
  9.8 24.0 %all-to-all-start = ((f32[16,5,8,256]{3,2,1,0:T(8,128)}), f32[16,5,8,256]{3,2,1,0:T(8,128)S(1)}, u32[]{:S(2)}, u32[]{:S(2)}) async-start(f32[16,5,8,256]{3,2,1,0:T(8,128)} %pad_maximum_fusion), calls=%async_computation | async-start | bytes 1310720 | tf_op jit(solution)/shard_map/all_to_all | solution.py:78
  17.2 139.4 %reduce-scatter.2.cloned.1.call-start = ((), (), s32[]{:S(2)}) async-start(), calls=%async_computation.2 | async-start | bytes 139264 | tf_op jit(solution)/shard_map/reduce_scatter | solution.py:158
  17.3 0.7 copy-start.2
  18.5 1.3 copy-start.3
  20.4 0.7 copy-start.4
  21.1 0.7 copy-start.5
  98.2 0.7 copy-start
  98.8 0.7 copy-start.1
Sparse Core Ops, SparseCore 0:
  103.7 52.8 reduce-scatter.1
where the time goes:
time: 164 us; the launch traced here: 163 us
  waiting for transfers between devices  63.8 us (39%)
  blocking collectives  60.8 us (37%)
  between operations  16.3 us (10%)
  other arithmetic  8.09 us (5%)
  starting transfers between devices  7.45 us (5%)
  local copies, waits for them, and re-layouts  7.03 us (4%)
    unnamed x1, blocking collectives  60.8 us
    reduce_scatter x1, waiting for transfers between devices, on_device(): gradient = lax.psum_scatter(gradient, 'kq', scatter_dimension=0, tiled=True)  53 us
    all_to_all x1, waiting for transfers between devices, on_device(): send = lax.all_to_all(send, 'kq', 0, 2, tiled=True)  10.8 us
    all_to_all x1, starting transfers between devices, on_device(): send = lax.all_to_all(send, 'kq', 0, 2, tiled=True)  7.41 us
    unnamed x14, local copies, waits for them, and re-layouts  3.66 us
  transfers between devices with their start and end apart: 2, of which 2 were waited for; matrix products, arithmetic and copies ran while one was open for 1% of the time, Pallas kernels for 0%

commit v1 on v0

--- a/solution.py
+++ b/solution.py
@@ -75,7 +75,10 @@
     sigma_copies = jnp.broadcast_to(conductivity[None, None], (groups, 1, own_columns, depth))
     send = jnp.concatenate([by_group(primary), by_group(prior_adjoint), sigma_copies], axis=1)
     if groups > 1:
-        send = lax.all_to_all(send, "kq", 0, 2, tiled=True)
+        send = jnp.concatenate(
+            lax.all_to_all(jnp.stack(jnp.split(send, lax.axis_size("kq"), axis=0)), "kq", 0, 0),
+            axis=2,
+        )
     received = send[0]
     width = groups * own_columns
     primary = received[:fields].reshape(per_group, sources, width, depth)

time: 164 us -> 173 us (1.055)
  local copies, waits for them, and re-layouts: 7.03 us -> 16.3 us
    unnamed x14 -> x29, local copies, waits for them, and re-layouts: 3.66 us -> 12.3 us
where the time goes in v1:
time: 173 us; the launch traced here: 172 us
  waiting for transfers between devices  64.4 us (37%)
  blocking collectives  60.8 us (35%)
  local copies, waits for them, and re-layouts  16.3 us (9%)
  between operations  16.3 us (9%)
  starting transfers between devices  7.45 us (4%)
  other arithmetic  7.24 us (4%)
    unnamed x1, blocking collectives  60.8 us
    reduce_scatter x1, waiting for transfers between devices, on_device(): gradient = lax.psum_scatter(gradient, 'kq', scatter_dimension=0, tiled=True)  53 us
    unnamed x29, local copies, waits for them, and re-layouts  12.3 us
    all_to_all x1, waiting for transfers between devices, on_device(): lax.all_to_all(jnp.stack(jnp.split(send, lax.axis_size('kq'), axis=0)), '...  11.4 us
    all_to_all x1, starting transfers between devices, on_device(): lax.all_to_all(jnp.stack(jnp.split(send, lax.axis_size('kq'), axis=0)), '...  7.41 us
  transfers between devices with their start and end apart: 2, of which 2 were waited for; matrix products, arithmetic and copies ran while one was open for 1% of the time, Pallas kernels for 0%

profile of v1, /device:TPU:0, one launch (start us, length us, event | category | flops | bytes accessed | tf_op | source)
XLA Modules:
  0.0 172.5 jit_solution(5868692386749008612)
XLA Ops:
  7.2 0.7 broadcast_in_dim.34
  7.9 1.1 pad_maximum_fusion
  9.0 0.6 fusion.76
  9.6 0.6 fusion.75
  10.2 0.6 fusion.74
  10.8 0.6 fusion.73
  11.4 0.6 fusion.72
  12.0 0.6 fusion.71
  12.6 0.6 fusion.70
  13.3 0.6 fusion.69
  13.9 0.6 fusion.68
  14.5 0.6 fusion.67
  15.1 0.6 fusion.66
  15.7 0.6 fusion.65
  16.3 0.6 fusion.64
  17.0 0.6 fusion.63
  17.6 0.6 fusion.62
  18.2 0.6 fusion.61
  18.8 7.4 %all-to-all-start = ((f32[16,1,5,8,256]{4,3,2,1,0:T(8,128)}), f32[16,1,5,8,256]{4,3,2,1,0:T(8,128)S(1)}, u32[]{:S(2)}, u32[]{:S(2)}) async-start(f32[16,1,5,8,256]{4,3,2,1,0:T(8,128)} %fusion.61), calls=%async_computation | async-start | bytes 1310720 | tf_op jit(solution)/shard_map/all_to_all | solution.py:79
  26.3 0.6 copy-done.2
  26.9 0.7 copy-done.3
  27.6 0.6 dynamic_slice.7
  29.5 0.6 dynamic_slice.6
  30.2 0.6 dynamic-slice
  31.4 11.4 %all-to-all-done = f32[16,1,5,8,256]{4,3,2,1,0:T(8,128)S(1)} async-done(((f32[16,1,5,8,256]{4,3,2,1,0:T(8,128)}), f32[16,1,5,8,256]{4,3,2,1,0:T(8,128)S(1)}, u32[]{:S(2)}, u32[]{:S(2)}) %all-to-all-start) | async-done | bytes 655392 | tf_op jit(solution)/shard_map/all_to_all | solution.py:79
  45.2 0.7 fusion.58
  46.1 60.8 %all-reduce.34 = f32[4128]{0:T(1024)S(1)} all-reduce(f32[4128]{0:T(1024)S(1)} %maximum_dynamic-update-slice_fusion), channel_id=2, replica_groups=mesh['lines'=2,'col'=16] {'col'}, use_global_device_ids=true, to_apply=%add.34 | all-reduce | flops 4128 | bytes 33024
  107.4 0.6 copy-done
  108.7 0.6 fusion.80
  109.4 0.6 broadcast_multiply_fusion.1
  111.8 0.8 add_reduce_fusion
  112.6 53.0 %reduce-scatter.2.cloned.1.call-done = f32[8,256]{1,0:T(8,128)} async-done(((f32[128,256]{1,0:T(8,128)}), f32[8,256]{1,0:T(8,128)}) %reduce-scatter.2.cloned.1.call-update) | async-done | bytes 8208 | tf_op jit(solution)/shard_map/reduce_scatter | solution.py:161
  (63 shorter events, 5.6 us)
Async XLA Ops:
  18.8 24.0 %all-to-all-start = ((f32[16,1,5,8,256]{4,3,2,1,0:T(8,128)}), f32[16,1,5,8,256]{4,3,2,1,0:T(8,128)S(1)}, u32[]{:S(2)}, u32[]{:S(2)}) async-start(f32[16,1,5,8,256]{4,3,2,1,0:T(8,128)} %fusion.61), calls=%async_computation | async-start | bytes 1310720 | tf_op jit(solution)/shard_map/all_to_all | solution.py:79
  26.2 139.4 %reduce-scatter.2.cloned.1.call-start = ((), (), s32[]{:S(2)}) async-start(), calls=%async_computation.2 | async-start | bytes 139264 | tf_op jit(solution)/shard_map/reduce_scatter | solution.py:161
  26.3 0.7 copy-start.2
  26.9 0.7 copy-start.3
  28.2 1.3 copy-start.4
  29.5 0.7 copy-start.5
  107.3 0.7 copy-start
  108.0 0.7 copy-start.1
Sparse Core Ops, SparseCore 0:
  112.7 52.8 reduce-scatter.1
